TPU v7x, 256 devices: a whole 4x4x8 slice. The times are simulated.
256 devices in a mesh: section: 4 (over z_lo, core), dp: 64 (over y, x, z_hi).
Axes of the slice: x: 4, y: 4, z: 8 (z_hi: 4, z_lo: 2; z = z_hi * 2 + z_lo), core: 2. Of those that a mesh axis runs over, the one named last changes fastest.
Arguments:
- activations_in: bfloat16 [2, 4096, 8192], P(None, 'dp'), may hold values from -6 to 6
- cotangent: bfloat16 [2, 4096, 8192], P(None, 'dp'), may hold values from -6 to 6
- value_tiles: bfloat16 [4, 128, 128, 128], P('section'), may hold values from -0.0625 to 0.0625
- value_ids: int32 [4, 128], P('section'), may hold values from 0 to 255, as said below
- out_tiles: bfloat16 [4, 192, 128, 128], P('section', 'dp'), may hold values from -0.25 to 0.25
- out_ids: int32 [4, 192], P('section'), may hold values from 0 to 255, as said below
- out_count: int32 [4, 64], P('section'), may hold values from 1 to 3, as said below
Outputs:
- section_outputs: bfloat16 [4, 2, 4096, 8192], P('section', None, 'dp')
- input_grads: bfloat16 [4, 2, 4096, 8192], P('section', None, 'dp')
- out_grad: float32 [4, 192, 128, 128], P('section', 'dp')
Inputs may be any that keep to these rules, and one draw needn't show every extreme that they name: `value_ids`: for each layer, 128 different tile numbers. `out_ids`: for each layer, 192 different tile numbers; slot g lies on index g // 3 of dp. The live slots of an index of dp are its first out_count slots; in each layer some index has all 3 slots live.
All inputs are finite; a program needn't handle non-finite values.
Results may differ from a plain program's by a relative error of at most 0.008.
Values may be sent and summed in bfloat16 or wider, within the bound.
No kernel may reach another device: no remote copies, remote signals or barrier semaphores. Data moves between devices by JAX's collectives and lax.ppermute only.
A program may use at most 192 MiB of HBM per device.

v0:
```python
import math
import jax
import jax.numpy as jnp
from jax import lax
from jax.sharding import PartitionSpec as P

VW = 512


def from_behind(value, axis, steps):
    count = lax.axis_size(axis)
    first, last = (max(0, -steps), min(count, count - steps))
    return lax.ppermute(value, axis, [(source, source + steps) for source in range(first, last)])


def build_blocks(tile_data, tile_ids, row_blocks, col_blocks):
    tile_width = tile_data.shape[-1]
    grid = jnp.zeros((row_blocks * col_blocks, tile_width, tile_width), jnp.bfloat16)
    grid = grid.at[tile_ids].set(tile_data)
    return grid.reshape(row_blocks, col_blocks, tile_width, tile_width)


def on_device(activations_in, cotangent, value_tiles, value_ids, out_tiles, out_ids, out_count):
    section_index = lax.axis_index("section")
    section_count = lax.axis_size("section")
    shard_count = lax.axis_size("dp")
    shard_index = lax.axis_index("dp")
    micro_count = activations_in.shape[0]
    tok_rows = activations_in.shape[1]
    model_width = activations_in.shape[2]
    all_rows = micro_count * tok_rows
    tile_width = value_tiles.shape[-1]
    value_width = VW
    value_blocks = value_width // tile_width
    model_blocks = model_width // tile_width
    slot_share = out_tiles.shape[1]
    out_slot = out_ids[0]
    live_mask = (jnp.arange(slot_share, dtype=jnp.int32)[None, :] < out_count[0][:, None]).reshape(
        -1
    )
    own_live = lax.dynamic_slice_in_dim(live_mask, shard_index * slot_share, slot_share)
    gathered = lax.all_gather(out_tiles[0], "dp", axis=0, tiled=True)
    masked_tiles = jnp.where(live_mask[:, None, None], gathered, jnp.zeros_like(gathered))
    value_grid = build_blocks(value_tiles[0], value_ids[0], model_blocks, value_blocks)
    out_grid = build_blocks(masked_tiles, out_slot, value_blocks, model_blocks)

    def forward_layer(operands):
        hidden, old_values, old_result = operands
        hidden_blocked = hidden.reshape(all_rows, model_blocks, tile_width)
        value_rows = jnp.einsum(
            "rbi,bvij->rvj", hidden_blocked, value_grid, preferred_element_type=jnp.float32
        ).astype(jnp.bfloat16)
        update = jnp.einsum(
            "rvi,vmij->rmj", value_rows, out_grid, preferred_element_type=jnp.float32
        ).reshape(all_rows, model_width)
        result = (hidden.astype(jnp.float32) + update).astype(jnp.bfloat16)
        return (value_rows.reshape(all_rows, value_width), result)

    def skip_forward(operands):
        return (operands[1], operands[2])

    def backward_layer(operands):
        grad_rows, old_input = operands
        grad_blocked = grad_rows.reshape(all_rows, model_blocks, tile_width)
        grad_values = jnp.einsum(
            "rmj,vmij->rvi", grad_blocked, out_grid, preferred_element_type=jnp.float32
        ).astype(jnp.bfloat16)
        extra_term = jnp.einsum(
            "rvj,bvij->rbi", grad_values, value_grid, preferred_element_type=jnp.float32
        ).reshape(all_rows, model_width)
        return (grad_rows.astype(jnp.float32) + extra_term).astype(jnp.bfloat16)

    def skip_backward(operands):
        return operands[1]

    first_input = activations_in.reshape(all_rows, model_width)
    value_store = jnp.zeros((all_rows, value_width), jnp.bfloat16)
    act_store = jnp.zeros((all_rows, model_width), jnp.bfloat16)
    carried = jnp.zeros((all_rows, model_width), jnp.bfloat16)
    for step_number in range(section_count):
        active = section_index == step_number
        hidden = jnp.where(section_index == 0, first_input, carried)
        value_store, act_store = lax.cond(
            active, forward_layer, skip_forward, (hidden, value_store, act_store)
        )
        if step_number + 1 < section_count:
            carried = from_behind(act_store, "section", 1)
    last_grad = cotangent.reshape(all_rows, model_width)
    grad_store = jnp.where(section_index == section_count - 1, last_grad, jnp.zeros_like(last_grad))
    input_store = jnp.zeros((all_rows, model_width), jnp.bfloat16)
    carried_grad = jnp.zeros((all_rows, model_width), jnp.bfloat16)
    for step_number in range(section_count):
        active = section_index == section_count - 1 - step_number
        if step_number > 0:
            grad_store = jnp.where(active, carried_grad, grad_store)
        input_store = lax.cond(active, backward_layer, skip_backward, (grad_store, input_store))
        if step_number + 1 < section_count:
            carried_grad = from_behind(input_store, "section", -1)
    grad_scale = 1.0 / math.sqrt(micro_count * tok_rows * shard_count)
    value_blocked = value_store.reshape(all_rows, value_blocks, tile_width)
    grad_blocked = grad_store.reshape(all_rows, model_blocks, tile_width)
    value_part = jnp.take(value_blocked, out_slot // model_blocks, axis=1)
    grad_part = jnp.take(grad_blocked, out_slot % model_blocks, axis=1)
    summed = lax.psum_scatter(
        jnp.einsum("rkc,rkd->kcd", value_part, grad_part, preferred_element_type=jnp.float32),
        "dp",
        scatter_dimension=0,
        tiled=True,
    )
    scaled = summed * grad_scale
    out_grad = jnp.where(own_live[:, None, None], scaled, jnp.zeros_like(scaled))
    section_out = act_store.reshape(micro_count, tok_rows, model_width)
    grad_out = input_store.reshape(micro_count, tok_rows, model_width)
    return (section_out[None], grad_out[None], out_grad[None])


def solution(mesh):
    in_specs = (
        P(None, "dp", None),
        P(None, "dp", None),
        P("section", None, None, None),
        P("section", None),
        P("section", "dp", None, None),
        P("section", None),
        P("section", None),
    )
    out_specs = (
        P("section", None, "dp", None),
        P("section", None, "dp", None),
        P("section", "dp", None, None),
    )
    return jax.shard_map(
        on_device, mesh=mesh, in_specs=in_specs, out_specs=out_specs, check_vma=False
    )
```

profile of v0, /device:TPU:2, one launch (start us, length us, event | category | flops | bytes accessed | tf_op | source)
XLA Modules:
  0.0 639.2 jit_solution(5982883603321064038)
XLA Ops:
  7.2 0.0 all-gather.3.cloned.1.call-start
  7.2 0.7 all-gather.3.cloned.1.call-update
  7.9 0.0 reduce-scatter.2.cloned.1.call-start
  8.0 0.7 iota_compare_fusion
  8.7 0.1 lt.107
  8.8 0.7 fusion.38
  9.5 5.4 broadcast.209.clone
  14.9 19.4 %scatter_fusion = bf16[256,128,128]{2,1,0:T(8,128)(2,1)} fusion(bf16[256,128,128]{2,1,0:T(8,128)(2,1)} %broadcast.209.clone, s32[128]{0:T(128)S(1)} %fusion.38, bf16[128,128,128]{2,1,0:T(8,128)(2,1)} %bitcast.307), kind=kCustom, calls=%fused_computation.2 | custom fusion | bytes 12583424 | tf_op jit(solution)/shard_map/scatter | solution.py:19
  34.3 0.1 broadcast_select_fusion.3
  34.5 78.6 %all-gather.3.cloned.1.call-done = bf16[1,192,128,128]{3,2,0,1:T(8,128)(2,1)} async-done(((bf16[1,3,128,128]{3,2,0,1:T(8,128)(2,1)}), bf16[1,192,128,128]{3,2,0,1:T(8,128)(2,1)}) %all-gather.3.cloned.1.call-update) | async-done | bytes 6291472 | tf_op jit(solution)/shard_map/all_gather | solution.py:42
  113.1 5.9 bitcast_select_fusion
  119.0 5.3 broadcast.209.clone.1
  124.3 28.7 %scatter_fusion.1 = bf16[256,128,128]{2,1,0:T(8,128)(2,1)} fusion(bf16[256,128,128]{2,1,0:T(8,128)(2,1)} %broadcast.209.clone.1, s32[192]{0:T(256)S(1)} %bitcast.312, bf16[192,128,128]{2,1,0:T(8,128)(2,1)} %bitcast_select_fusion), kind=kCustom, calls=%fused_computation.3 | custom fusion | bytes 18875136 | tf_op jit(solution)/shard_map/scatter | solution.py:19
  153.1 0.0 copy-done.8
  153.1 1.6 conditional.12
  153.1 1.6 broadcast.201
  154.7 4.2 copy.131
  158.9 1.3 collective-permute-start.3
  160.2 1.6 broadcast_select_fusion.7
  161.8 18.7 %conditional.8 = (bf16[128,512]{0,1:T(8,128)(2,1)}, bf16[128,8192]{0,1:T(8,128)(2,1)}) conditional(s32[]{:T(128)} %convert_element_type.91, () %tuple.76, (bf16[128,8192]{1,0:T(8,128)(2,1)}, bf16[64,4,128,128]{3,2,1,0:T(8,128)(2,1)}, bf16[4,64,128,128]{3,2,1,0:T(8,128)(2,1)}) %tuple.158), branch_computations={%region_2.3_spmd, %region_3.4_spmd} | conditional | flops 2150694912 | bytes 77856840 | solution.py:83
  162.0 4.1 copy.115
  166.1 8.2 %fusion.1 = bf16[128,4,128]{0,2,1:T(8,128)(2,1)} fusion(bf16[128,64,128,1]{0,2,3,1:T(8,128)(2,1)} %bitcast.306, bf16[64,4,128,128]{3,2,1,0:T(8,128)(2,1)} %get-tuple-element.207), kind=kOutput, calls=%fused_computation.7 | convolution fusion | flops 1073807360 | bytes 10616832 | tf_op jit(solution)/shard_map/cond/branch_1_fun/rbi,bvij->rvj/dot_general | solution.py:50
  174.3 4.4 fusion.2
  178.7 1.8 fusion
  180.5 4.1 copy.118
  184.5 2.6 collective-permute-start
  187.2 0.0 collective-permute-done.3
  187.2 3.1 broadcast_select_fusion.2
  190.3 4.1 copy.133
  194.4 1.3 collective-permute-start.4
  195.7 0.0 collective-permute-done
  195.7 1.7 broadcast_select_fusion.6
  197.4 0.4 conditional.9
  197.8 4.1 copy.122
  201.9 25.1 %collective-permute-start.1 = (bf16[128,8192]{1,0:T(8,128)(2,1)}, bf16[128,8192]{1,0:T(8,128)(2,1)}, u32[]{:S(2)}, u32[]{:S(2)}) collective-permute-start(bf16[128,8192]{1,0:T(8,128)(2,1)} %copy.122), channel_id=1, source_target_pairs={{0,64},{64,128},{128,192},{1,65},{65,129},{129,193},{2,66},{66,130... | collective-permute-start | bytes 6291464 | tf_op jit(solution)/shard_map/ppermute | solution.py:13
  227.0 0.0 collective-permute-done.4
  227.0 3.1 broadcast_select_fusion.1
  230.1 4.2 conditional.14
  230.1 4.1 copy.191
  234.4 1.3 collective-permute-start.5
  235.7 0.0 collective-permute-done.1
  235.7 29.9 %collective-permute-done.5 = bf16[128,8192]{1,0:T(8,128)(2,1)S(1)} collective-permute-done((bf16[128,8192]{1,0:T(8,128)(2,1)}, bf16[128,8192]{1,0:T(8,128)(2,1)S(1)}, u32[]{:S(2)}, u32[]{:S(2)}) %collective-permute-start.5) | collective-permute-done | bytes 2097184 | tf_op jit(solution)/shard_map/ppermute | solution.py:13
  265.6 2.6 broadcast_select_fusion.4
  268.2 0.2 conditional.10
  268.4 27.1 %collective-permute-start.2 = (bf16[128,8192]{0,1:T(8,128)(2,1)}, bf16[128,8192]{0,1:T(8,128)(2,1)}, u32[]{:S(2)}, u32[]{:S(2)}) collective-permute-start(bf16[128,8192]{0,1:T(8,128)(2,1)} %get-tuple-element.131), channel_id=1, source_target_pairs={{0,64},{64,128},{128,192},{1,65},{65,129},{129,193},{2,66},{66,130... | collective-permute-start | bytes 6291464 | tf_op jit(solution)/shard_map/ppermute | solution.py:13
  295.6 4.1 copy.137
  299.6 4.1 copy.138
  303.7 9.6 %gather_fusion.1 = bf16[192,128,128]{2,1,0:T(8,128)(2,1)} fusion(bf16[128,64,128]{2,0,1:T(8,128)(2,1)} %copy.138, s32[1024]{0:T(1024)S(1)} %pad_clamp_fusion), kind=kCustom, calls=%fused_computation.1 | custom fusion | bytes 12583680 | tf_op jit(solution)/shard_map/jit(_take)/gather | solution.py:103
  313.3 0.0 collective-permute-done.2
  313.3 1.9 conditional.11
  313.3 1.6 copy.107
  315.2 8.8 %gather_fusion = bf16[192,128,128]{2,1,0:T(8,128)(2,1)} fusion(bf16[128,4,128]{2,0,1:T(8,128)(2,1)} %get-tuple-element.133, s32[1024]{0:T(1024)S(1)} %pad_clamp_fusion.1), kind=kCustom, calls=%fused_computation | custom fusion | bytes 12583680 | tf_op jit(solution)/shard_map/jit(_take)/gather | solution.py:102
  324.0 11.8 %fusion.30 = f32[192,128,128]{2,1,0:T(8,128)} fusion(bf16[192,128,128]{2,1,0:T(8,128)(2,1)} %gather_fusion.1, bf16[192,128,128]{2,1,0:T(8,128)(2,1)} %gather_fusion, pred[192]{0:T(512)(128)(4,1)S(1)} %get-tuple-element.233, pred[192]{0:T(512)(128)(4,1)S(1)} %get-tuple-element.232), kind=kOutput, calls=%fused_computation.51 | convolution fusion | flops 811597824 | bytes 25166208 | tf_op jit(solution)/shard_map/rkc,rkd->kcd/dot_general | solution.py:105
  335.8 0.0 reduce-scatter.2.cloned.1.call-update
  335.8 0.1 dynamic_slice.3
  335.9 1.5 copy-done.9
  337.3 20.5 %conditional.15 = (bf16[1,2,64,8192]{3,2,1,0:T(8,128)(2,1)}) conditional(s32[]{:T(128)} %convert_element_type.91, bf16[128,8192]{1,0:T(8,128)(2,1)} %get-tuple-element.229, (bf16[128,8192]{1,0:T(8,128)(2,1)S(1)}, bf16[4,64,128,128]{3,2,1,0:T(8,128)(2,1)}, bf16[64,4,128,128]{3,2,1,0:T(8,128)(2,1)}) %tuple.167), branch_computations={%region_16.17_spmd, %region_17.18_spmd} | conditional | flops 2150694912 | bytes 73662504 | solution.py:96
  337.6 6.4 fusion.29
  344.0 4.3 fusion.43
  348.3 5.6 copy.113
  354.0 3.9 add_convert_fusion
  357.9 4.1 copy.129
  362.0 268.2 %reduce-scatter.2.cloned.1.call-done = f32[3,128,128]{2,1,0:T(8,128)} async-done(((f32[192,128,128]{2,1,0:T(8,128)}), f32[3,128,128]{2,1,0:T(8,128)}) %reduce-scatter.2.cloned.1.call-update) | async-done | bytes 196624 | tf_op jit(solution)/shard_map/reduce_scatter | solution.py:104
  630.2 1.7 select_bitcast_fusion
  (18 shorter events, 0.1 us)
Async XLA Ops:
  7.2 105.9 %all-gather.3.cloned.1.call-start = ((), (), s32[]{:S(2)}) async-start(), calls=%async_computation.2 | async-start | bytes 6389760 | tf_op jit(solution)/shard_map/all_gather | solution.py:42
  7.9 622.3 %reduce-scatter.2.cloned.1.call-start = ((), (), s32[]{:S(2)}) async-start(), calls=%async_computation.1 | async-start | bytes 12779520 | tf_op jit(solution)/shard_map/reduce_scatter | solution.py:104
  14.9 19.4 %copy-start.16 = (s32[1,192]{1,0:T(1,128)S(1)}, s32[1,192]{1,0:T(1,128)}, u32[]{:S(2)}) copy-start(s32[1,192]{1,0:T(1,128)} %param.28) | copy-start | bytes 2308
  34.4 118.6 %copy-start.8 = (bf16[2,64,8192]{2,1,0:T(8,128)(2,1)}, bf16[2,64,8192]{2,1,0:T(8,128)(2,1)S(1)}, u32[]{:S(2)}) copy-start(bf16[2,64,8192]{2,1,0:T(8,128)(2,1)S(1)} %broadcast_select_fusion.3) | copy-start | bytes 6291460
  154.7 5.5 copy-start.7
  158.9 28.3 %collective-permute-start.3 = (bf16[128,8192]{1,0:T(8,128)(2,1)}, bf16[128,8192]{1,0:T(8,128)(2,1)}, u32[]{:S(2)}, u32[]{:S(2)}) collective-permute-start(bf16[128,8192]{1,0:T(8,128)(2,1)} %copy.131), channel_id=1, source_target_pairs={{64,0},{128,64},{192,128},{65,1},{129,65},{193,129},{66,2},{130,66... | collective-permute-start | bytes 6291464 | tf_op jit(solution)/shard_map/ppermute | solution.py:13
  166.1 8.2 %copy-start.4 = (bf16[4,64,128,128]{3,2,1,0:T(8,128)(2,1)S(1)}, bf16[4,64,128,128]{3,2,1,0:T(8,128)(2,1)}, u32[]{:S(2)}) copy-start(bf16[4,64,128,128]{3,2,1,0:T(8,128)(2,1)} %get-tuple-element.208) | copy-start | bytes 25165828 | tf_op jit(solution)/shard_map/cond
  174.3 4.4 copy-start.15
  184.5 11.2 %collective-permute-start = (bf16[128,8192]{1,0:T(8,128)(2,1)}, bf16[128,8192]{1,0:T(8,128)(2,1)}, u32[]{:S(2)}, u32[]{:S(2)}) collective-permute-start(bf16[128,8192]{1,0:T(8,128)(2,1)} %copy.118), channel_id=1, source_target_pairs={{0,64},{64,128},{128,192},{1,65},{65,129},{129,193},{2,66},{66,130... | collective-permute-start | bytes 6291464 | tf_op jit(solution)/shard_map/ppermute | solution.py:13
  194.4 32.6 %collective-permute-start.4 = (bf16[128,8192]{1,0:T(8,128)(2,1)}, bf16[128,8192]{1,0:T(8,128)(2,1)}, u32[]{:S(2)}, u32[]{:S(2)}) collective-permute-start(bf16[128,8192]{1,0:T(8,128)(2,1)} %copy.133), channel_id=1, source_target_pairs={{64,0},{128,64},{192,128},{65,1},{129,65},{193,129},{66,2},{130,66... | collective-permute-start | bytes 6291464 | tf_op jit(solution)/shard_map/ppermute | solution.py:13
  201.9 33.8 %collective-permute-start.1 = (bf16[128,8192]{1,0:T(8,128)(2,1)}, bf16[128,8192]{1,0:T(8,128)(2,1)}, u32[]{:S(2)}, u32[]{:S(2)}) collective-permute-start(bf16[128,8192]{1,0:T(8,128)(2,1)} %copy.122), channel_id=1, source_target_pairs={{0,64},{64,128},{128,192},{1,65},{65,129},{129,193},{2,66},{66,130... | collective-permute-start | bytes 6291464 | tf_op jit(solution)/shard_map/ppermute | solution.py:13
  234.4 31.2 %collective-permute-start.5 = (bf16[128,8192]{1,0:T(8,128)(2,1)}, bf16[128,8192]{1,0:T(8,128)(2,1)S(1)}, u32[]{:S(2)}, u32[]{:S(2)}) collective-permute-start(bf16[128,8192]{1,0:T(8,128)(2,1)} %get-tuple-element.229), channel_id=1, source_target_pairs={{64,0},{128,64},{192,128},{65,1},{129,65},{193,129},{66,2},{130,66... | collective-permute-start | bytes 6291464 | tf_op jit(solution)/shard_map/ppermute | solution.py:13
  268.4 44.9 %collective-permute-start.2 = (bf16[128,8192]{0,1:T(8,128)(2,1)}, bf16[128,8192]{0,1:T(8,128)(2,1)}, u32[]{:S(2)}, u32[]{:S(2)}) collective-permute-start(bf16[128,8192]{0,1:T(8,128)(2,1)} %get-tuple-element.131), channel_id=1, source_target_pairs={{0,64},{64,128},{128,192},{1,65},{65,129},{129,193},{2,66},{66,130... | collective-permute-start | bytes 6291464 | tf_op jit(solution)/shard_map/ppermute | solution.py:13
  335.7 1.6 copy-start.9
  337.6 6.4 copy-start.3
Sparse Core Ops, SparseCore 0:
  11.2 101.7 all-gather.2
  335.9 294.2 reduce-scatter.1
where the time goes:
time: 648 us; the launch traced here: 639 us
  waiting for transfers between devices  377 us (58%)
  local copies, waits for them, and re-layouts  125 us (19%)
  starting transfers between devices  58.8 us (9%)
  matrix products  35 us (5%)
  other arithmetic  27 us (4%)
  between operations  14.7 us (2%)
    reduce_scatter x1, waiting for transfers between devices, on_device(): lax.psum_scatter(jnp.einsum('rkc,rkd->kcd', value_part, grad_part, prefer...  268 us
    all_gather x1, waiting for transfers between devices, on_device(): gathered = lax.all_gather(out_tiles[0], 'dp', axis=0, tiled=True)  78.6 us
    ppermute x6, starting transfers between devices, from_behind(): lax.ppermute(value, axis, [(source, source + steps) for source in range(f...  58.7 us
    scatter x2, local copies, waits for them, and re-layouts, build_blocks(): grid = grid.at[tile_ids].set(tile_data)  48.1 us
    ppermute x6, waiting for transfers between devices, from_behind(): lax.ppermute(value, axis, [(source, source + steps) for source in range(f...  29.9 us
    another operation x5, local copies, waits for them, and re-layouts  18.1 us
  transfers between devices with their start and end apart: 8, of which 3 were waited for; matrix products, arithmetic and copies ran while one was open for 18% of the time, Pallas kernels for 0%

commit v1 on v0

--- a/solution.py
+++ b/solution.py
@@ -39,7 +39,9 @@
         -1
     )
     own_live = lax.dynamic_slice_in_dim(live_mask, shard_index * slot_share, slot_share)
-    gathered = lax.all_gather(out_tiles[0], "dp", axis=0, tiled=True)
+    gathered = jnp.concatenate(
+        lax.all_to_all(jnp.stack([out_tiles[0]] * lax.axis_size("dp")), "dp", 0, 0), axis=0
+    )
     masked_tiles = jnp.where(live_mask[:, None, None], gathered, jnp.zeros_like(gathered))
     value_grid = build_blocks(value_tiles[0], value_ids[0], model_blocks, value_blocks)
     out_grid = build_blocks(masked_tiles, out_slot, value_blocks, model_blocks)

time: 648 us -> 701 us (1.082)
  waiting for transfers between devices: 377 us -> 411 us
  starting transfers between devices: 58.8 us -> 72.9 us
    all_to_all x0 -> x1, waiting for transfers between devices: none -> 117 us  [on_device(): lax.all_to_all(jnp.stack([out_tiles[0]] * lax.axis_size('dp')), 'dp', 0, 0)]
    all_gather x1 -> x0, waiting for transfers between devices: 78.6 us -> none  [on_device(): gathered = lax.all_gather(out_tiles[0], 'dp', axis=0, tiled=True)]
    all_to_all x0 -> x1, starting transfers between devices: none -> 14.9 us  [on_device(): lax.all_to_all(jnp.stack([out_tiles[0]] * lax.axis_size('dp')), 'dp', 0, 0)]
    another operation x5 -> x6, local copies, waits for them, and re-layouts: 18.1 us -> 23.3 us
  transfers between devices with their start and end apart: 8 -> 8, of which waited for: 3 -> 3; matrix products, arithmetic and copies ran while one was open for 18% -> 16% of each run, Pallas kernels for 0% -> 0%
where the time goes in v1:
time: 701 us; the launch traced here: 691 us
  waiting for transfers between devices  411 us (59%)
  local copies, waits for them, and re-layouts  130 us (19%)
  starting transfers between devices  72.9 us (10%)
  matrix products  35.1 us (5%)
  other arithmetic  25.7 us (4%)
  between operations  14.7 us (2%)
    reduce_scatter x1, waiting for transfers between devices, on_device(): lax.psum_scatter(jnp.einsum('rkc,rkd->kcd', value_part, grad_part, prefer...  266 us
    all_to_all x1, waiting for transfers between devices, on_device(): lax.all_to_all(jnp.stack([out_tiles[0]] * lax.axis_size('dp')), 'dp', 0, 0)  117 us
    ppermute x6, starting transfers between devices, from_behind(): lax.ppermute(value, axis, [(source, source + steps) for source in range(f...  57.9 us
    scatter x2, local copies, waits for them, and re-layouts, build_blocks(): grid = grid.at[tile_ids].set(tile_data)  48.7 us
    ppermute x6, waiting for transfers between devices, from_behind(): lax.ppermute(value, axis, [(source, source + steps) for source in range(f...  27.5 us
    another operation x5, local copies, waits for them, and re-layouts  18.1 us
    all_to_all x1, starting transfers between devices, on_device(): lax.all_to_all(jnp.stack([out_tiles[0]] * lax.axis_size('dp')), 'dp', 0, 0)  14.9 us
  transfers between devices with their start and end apart: 8, of which 3 were waited for; matrix products, arithmetic and copies ran while one was open for 16% of the time, Pallas kernels for 0%

profile of v1, /device:TPU:2, one launch (start us, length us, event | category | flops | bytes accessed | tf_op | source)
XLA Modules:
  0.0 690.8 jit_solution(8522582110993664583)
XLA Ops:
  7.2 5.2 stack.3
  12.3 14.9 %all-to-all-start = ((bf16[64,3,128,128]{3,2,1,0:T(8,128)(2,1)}), bf16[64,3,128,128]{3,2,1,0:T(8,128)(2,1)}, u32[]{:S(2)}, u32[]{:S(2)}) async-start(bf16[64,3,128,128]{3,2,1,0:T(8,128)(2,1)} %stack.3), calls=%async_computation | async-start | bytes 12582912 | tf_op jit(solution)/shard_map/all_to_all | solution.py:43
  27.3 0.0 reduce-scatter.2.cloned.1.call-start
  27.3 0.0 copy-done.17
  27.3 0.1 iota_compare_fusion
  27.4 0.2 lt.107
  27.6 0.0 copy-done.18
  27.6 5.4 broadcast.210.clone
  33.0 19.5 %scatter_fusion = bf16[256,128,128]{2,1,0:T(8,128)(2,1)} fusion(bf16[256,128,128]{2,1,0:T(8,128)(2,1)} %broadcast.210.clone, s32[128]{0:T(128)S(1)} %fusion.38, bf16[128,128,128]{2,1,0:T(8,128)(2,1)} %bitcast.307), kind=kCustom, calls=%fused_computation.2 | custom fusion | bytes 12583424 | tf_op jit(solution)/shard_map/scatter | solution.py:19
  52.6 0.1 broadcast_select_fusion.3
  52.7 117.0 %all-to-all-done = bf16[64,3,128,128]{3,2,1,0:T(8,128)(2,1)} async-done(((bf16[64,3,128,128]{3,2,1,0:T(8,128)(2,1)}), bf16[64,3,128,128]{3,2,1,0:T(8,128)(2,1)}, u32[]{:S(2)}, u32[]{:S(2)}) %all-to-all-start) | async-done | bytes 6291488 | tf_op jit(solution)/shard_map/all_to_all | solution.py:43
  169.8 6.0 bitcast_select_fusion
  175.8 5.3 broadcast.210.clone.1
  181.1 29.1 %scatter_fusion.1 = bf16[256,128,128]{2,1,0:T(8,128)(2,1)} fusion(bf16[256,128,128]{2,1,0:T(8,128)(2,1)} %broadcast.210.clone.1, s32[192]{0:T(256)S(1)} %bitcast.312, bf16[192,128,128]{2,1,0:T(8,128)(2,1)} %bitcast_select_fusion), kind=kCustom, calls=%fused_computation.3 | custom fusion | bytes 18875136 | tf_op jit(solution)/shard_map/scatter | solution.py:19
  210.2 1.6 conditional.12
  210.2 1.6 broadcast.202
  211.8 4.2 copy.92
  216.0 1.3 collective-permute-start.3
  217.3 1.6 broadcast_select_fusion.7
  218.9 18.7 %conditional.8 = (bf16[128,512]{0,1:T(8,128)(2,1)}, bf16[128,8192]{0,1:T(8,128)(2,1)}) conditional(s32[]{:T(128)} %convert_element_type.91, () %tuple.76, (bf16[128,8192]{1,0:T(8,128)(2,1)}, bf16[64,4,128,128]{3,2,1,0:T(8,128)(2,1)}, bf16[4,64,128,128]{3,2,1,0:T(8,128)(2,1)}) %tuple.148), branch_computations={%region_2.3_spmd, %region_3.4_spmd} | conditional | flops 2150694912 | bytes 77856840 | solution.py:85
  219.1 4.1 copy.76
  223.2 8.2 %fusion.1 = bf16[128,4,128]{0,2,1:T(8,128)(2,1)} fusion(bf16[128,64,128,1]{0,2,3,1:T(8,128)(2,1)} %bitcast.306, bf16[64,4,128,128]{3,2,1,0:T(8,128)(2,1)} %get-tuple-element.182), kind=kOutput, calls=%fused_computation.7 | convolution fusion | flops 1073807360 | bytes 10616832 | tf_op jit(solution)/shard_map/cond/branch_1_fun/rbi,bvij->rvj/dot_general | solution.py:52
  231.4 4.4 fusion.2
  235.8 1.8 fusion
  237.6 4.1 copy.79
  241.7 2.6 collective-permute-start
  244.3 0.0 collective-permute-done.3
  244.3 3.1 broadcast_select_fusion.2
  247.4 4.1 copy.94
  251.5 1.3 collective-permute-start.4
  252.8 0.0 collective-permute-done
  252.8 1.7 broadcast_select_fusion.6
  254.5 0.4 conditional.9
  254.9 4.1 copy.83
  259.0 24.3 %collective-permute-start.1 = (bf16[128,8192]{1,0:T(8,128)(2,1)}, bf16[128,8192]{1,0:T(8,128)(2,1)}, u32[]{:S(2)}, u32[]{:S(2)}) collective-permute-start(bf16[128,8192]{1,0:T(8,128)(2,1)} %copy.83), channel_id=1, source_target_pairs={{0,64},{64,128},{128,192},{1,65},{65,129},{129,193},{2,66},{66,130... | collective-permute-start | bytes 6291464 | tf_op jit(solution)/shard_map/ppermute | solution.py:13
  283.3 0.0 collective-permute-done.4
  283.3 3.1 broadcast_select_fusion.1
  286.4 4.2 conditional.14
  286.4 4.1 copy.152
  290.7 1.3 collective-permute-start.5
  292.0 0.0 collective-permute-done.1
  292.0 27.5 %collective-permute-done.5 = bf16[128,8192]{1,0:T(8,128)(2,1)S(1)} collective-permute-done((bf16[128,8192]{1,0:T(8,128)(2,1)}, bf16[128,8192]{1,0:T(8,128)(2,1)S(1)}, u32[]{:S(2)}, u32[]{:S(2)}) %collective-permute-start.5) | collective-permute-done | bytes 2097184 | tf_op jit(solution)/shard_map/ppermute | solution.py:13
  319.5 2.6 broadcast_select_fusion.4
  322.0 0.2 conditional.10
  322.2 27.1 %collective-permute-start.2 = (bf16[128,8192]{0,1:T(8,128)(2,1)}, bf16[128,8192]{0,1:T(8,128)(2,1)}, u32[]{:S(2)}, u32[]{:S(2)}) collective-permute-start(bf16[128,8192]{0,1:T(8,128)(2,1)} %get-tuple-element.131), channel_id=1, source_target_pairs={{0,64},{64,128},{128,192},{1,65},{65,129},{129,193},{2,66},{66,130... | collective-permute-start | bytes 6291464 | tf_op jit(solution)/shard_map/ppermute | solution.py:13
  349.4 4.1 copy.98
  353.5 4.1 copy.99
  357.6 9.6 %gather_fusion.1 = bf16[192,128,128]{2,1,0:T(8,128)(2,1)} fusion(bf16[128,64,128]{2,0,1:T(8,128)(2,1)} %copy.99, s32[1024]{0:T(1024)S(1)} %pad_clamp_fusion), kind=kCustom, calls=%fused_computation.1 | custom fusion | bytes 12583680 | tf_op jit(solution)/shard_map/jit(_take)/gather | solution.py:105
  367.2 0.0 collective-permute-done.2
  367.2 1.9 conditional.11
  367.2 1.7 copy.69
  369.1 8.8 %gather_fusion = bf16[192,128,128]{2,1,0:T(8,128)(2,1)} fusion(bf16[128,4,128]{2,0,1:T(8,128)(2,1)} %get-tuple-element.133, s32[1024]{0:T(1024)S(1)} %pad_clamp_fusion.1), kind=kCustom, calls=%fused_computation | custom fusion | bytes 12583680 | tf_op jit(solution)/shard_map/jit(_take)/gather | solution.py:104
  377.9 11.8 %fusion.30 = f32[192,128,128]{2,1,0:T(8,128)} fusion(bf16[192,128,128]{2,1,0:T(8,128)(2,1)} %gather_fusion.1, bf16[192,128,128]{2,1,0:T(8,128)(2,1)} %gather_fusion, pred[192]{0:T(512)(128)(4,1)S(1)} %get-tuple-element.208, pred[192]{0:T(512)(128)(4,1)S(1)} %get-tuple-element.207), kind=kOutput, calls=%fused_computation.51 | convolution fusion | flops 811597824 | bytes 25166208 | tf_op jit(solution)/shard_map/rkc,rkd->kcd/dot_general | solution.py:107
  389.6 0.0 reduce-scatter.2.cloned.1.call-update
  389.7 0.1 dynamic_slice.3
  389.8 1.5 copy-done.9
  391.2 20.5 %conditional.15 = (bf16[1,2,64,8192]{3,2,1,0:T(8,128)(2,1)}) conditional(s32[]{:T(128)} %convert_element_type.91, bf16[128,8192]{1,0:T(8,128)(2,1)} %get-tuple-element.204, (bf16[128,8192]{1,0:T(8,128)(2,1)S(1)}, bf16[4,64,128,128]{3,2,1,0:T(8,128)(2,1)}, bf16[64,4,128,128]{3,2,1,0:T(8,128)(2,1)}) %tuple.157), branch_computations={%region_16.17_spmd, %region_17.18_spmd} | conditional | flops 2150694912 | bytes 73662504 | solution.py:98
  391.5 6.4 fusion.29
  397.9 4.3 fusion.43
  402.2 5.6 copy.75
  407.8 3.9 add_convert_fusion
  411.7 4.1 copy.90
  415.8 266.0 %reduce-scatter.2.cloned.1.call-done = f32[3,128,128]{2,1,0:T(8,128)} async-done(((f32[192,128,128]{2,1,0:T(8,128)}), f32[3,128,128]{2,1,0:T(8,128)}) %reduce-scatter.2.cloned.1.call-update) | async-done | bytes 196624 | tf_op jit(solution)/shard_map/reduce_scatter | solution.py:106
  681.8 1.7 select_bitcast_fusion
  (22 shorter events, 0.1 us)
Async XLA Ops:
  12.3 15.0 %copy-start.17 = (s32[1,64]{1,0:T(1,128)S(1)}, s32[1,64]{1,0:T(1,128)}, u32[]{:S(2)}) copy-start(s32[1,64]{1,0:T(1,128)} %param.29) | copy-start | bytes 772
  12.3 15.3 %copy-start.18 = (s32[1,128]{1,0:T(1,128)S(1)}, s32[1,128]{1,0:T(1,128)}, u32[]{:S(2)}) copy-start(s32[1,128]{1,0:T(1,128)} %param.26) | copy-start | bytes 1540
  12.3 157.5 %all-to-all-start = ((bf16[64,3,128,128]{3,2,1,0:T(8,128)(2,1)}), bf16[64,3,128,128]{3,2,1,0:T(8,128)(2,1)}, u32[]{:S(2)}, u32[]{:S(2)}) async-start(bf16[64,3,128,128]{3,2,1,0:T(8,128)(2,1)} %stack.3), calls=%async_computation | async-start | bytes 12582912 | tf_op jit(solution)/shard_map/all_to_all | solution.py:43
  27.3 654.5 %reduce-scatter.2.cloned.1.call-start = ((), (), s32[]{:S(2)}) async-start(), calls=%async_computation.2 | async-start | bytes 12779520 | tf_op jit(solution)/shard_map/reduce_scatter | solution.py:106
  33.0 19.5 %copy-start.16 = (s32[1,192]{1,0:T(1,128)S(1)}, s32[1,192]{1,0:T(1,128)}, u32[]{:S(2)}) copy-start(s32[1,192]{1,0:T(1,128)} %param.28) | copy-start | bytes 2308
  52.7 157.5 %copy-start.8 = (bf16[2,64,8192]{2,1,0:T(8,128)(2,1)}, bf16[2,64,8192]{2,1,0:T(8,128)(2,1)S(1)}, u32[]{:S(2)}) copy-start(bf16[2,64,8192]{2,1,0:T(8,128)(2,1)S(1)} %broadcast_select_fusion.3) | copy-start | bytes 6291460
  211.8 5.5 copy-start.7
  216.0 28.3 %collective-permute-start.3 = (bf16[128,8192]{1,0:T(8,128)(2,1)}, bf16[128,8192]{1,0:T(8,128)(2,1)}, u32[]{:S(2)}, u32[]{:S(2)}) collective-permute-start(bf16[128,8192]{1,0:T(8,128)(2,1)} %copy.92), channel_id=1, source_target_pairs={{64,0},{128,64},{192,128},{65,1},{129,65},{193,129},{66,2},{130,66... | collective-permute-start | bytes 6291464 | tf_op jit(solution)/shard_map/ppermute | solution.py:13
  223.2 8.2 %copy-start.4 = (bf16[4,64,128,128]{3,2,1,0:T(8,128)(2,1)S(1)}, bf16[4,64,128,128]{3,2,1,0:T(8,128)(2,1)}, u32[]{:S(2)}) copy-start(bf16[4,64,128,128]{3,2,1,0:T(8,128)(2,1)} %get-tuple-element.183) | copy-start | bytes 25165828 | tf_op jit(solution)/shard_map/cond
  231.4 4.4 copy-start.15
  241.7 11.2 %collective-permute-start = (bf16[128,8192]{1,0:T(8,128)(2,1)}, bf16[128,8192]{1,0:T(8,128)(2,1)}, u32[]{:S(2)}, u32[]{:S(2)}) collective-permute-start(bf16[128,8192]{1,0:T(8,128)(2,1)} %copy.79), channel_id=1, source_target_pairs={{0,64},{64,128},{128,192},{1,65},{65,129},{129,193},{2,66},{66,130... | collective-permute-start | bytes 6291464 | tf_op jit(solution)/shard_map/ppermute | solution.py:13
  251.5 31.8 %collective-permute-start.4 = (bf16[128,8192]{1,0:T(8,128)(2,1)}, bf16[128,8192]{1,0:T(8,128)(2,1)}, u32[]{:S(2)}, u32[]{:S(2)}) collective-permute-start(bf16[128,8192]{1,0:T(8,128)(2,1)} %copy.94), channel_id=1, source_target_pairs={{64,0},{128,64},{192,128},{65,1},{129,65},{193,129},{66,2},{130,66... | collective-permute-start | bytes 6291464 | tf_op jit(solution)/shard_map/ppermute | solution.py:13
  259.0 32.9 %collective-permute-start.1 = (bf16[128,8192]{1,0:T(8,128)(2,1)}, bf16[128,8192]{1,0:T(8,128)(2,1)}, u32[]{:S(2)}, u32[]{:S(2)}) collective-permute-start(bf16[128,8192]{1,0:T(8,128)(2,1)} %copy.83), channel_id=1, source_target_pairs={{0,64},{64,128},{128,192},{1,65},{65,129},{129,193},{2,66},{66,130... | collective-permute-start | bytes 6291464 | tf_op jit(solution)/shard_map/ppermute | solution.py:13
  290.7 28.8 %collective-permute-start.5 = (bf16[128,8192]{1,0:T(8,128)(2,1)}, bf16[128,8192]{1,0:T(8,128)(2,1)S(1)}, u32[]{:S(2)}, u32[]{:S(2)}) collective-permute-start(bf16[128,8192]{1,0:T(8,128)(2,1)} %get-tuple-element.204), channel_id=1, source_target_pairs={{64,0},{128,64},{192,128},{65,1},{129,65},{193,129},{66,2},{130,66... | collective-permute-start | bytes 6291464 | tf_op jit(solution)/shard_map/ppermute | solution.py:13
  322.2 44.9 %collective-permute-start.2 = (bf16[128,8192]{0,1:T(8,128)(2,1)}, bf16[128,8192]{0,1:T(8,128)(2,1)}, u32[]{:S(2)}, u32[]{:S(2)}) collective-permute-start(bf16[128,8192]{0,1:T(8,128)(2,1)} %get-tuple-element.131), channel_id=1, source_target_pairs={{0,64},{64,128},{128,192},{1,65},{65,129},{129,193},{2,66},{66,130... | collective-permute-start | bytes 6291464 | tf_op jit(solution)/shard_map/ppermute | solution.py:13
  389.6 1.6 copy-start.9
  391.5 6.4 copy-start.3
Sparse Core Ops, SparseCore 0:
  389.8 291.9 reduce-scatter.1
